TPU v7x, 256 devices: a whole 4x4x8 slice. The times are simulated.
256 devices in a mesh: blk: 64 (over y, x_lo, z), team: 4 (over x_hi, core).
Axes of the slice: x: 4 (x_hi: 2, x_lo: 2; x = x_hi * 2 + x_lo), y: 4, z: 8, core: 2. Of those that a mesh axis runs over, the one named last changes fastest.
Arguments:
- loadings: bfloat16 [64, 98304], P(None, ('blk', 'team')), may hold values from -6 to 6
- scales: bfloat16 [64, 768], P(None, ('blk', 'team')), may hold values from 0.25 to 4
- cov: bfloat16 [16384, 16, 4, 1536], P('blk', None, 'team'), may hold values from -0.01953125 to 0.01953125
Outputs:
- product: float32 [64, 16384], P(None, 'blk')
All inputs are finite; a program needn't handle non-finite values.
Results may differ from a plain program's by a relative error of at most 0.0028.
Values may be sent and summed in bfloat16 or wider, within the bound.
No kernel may reach another device: no remote copies, remote signals or barrier semaphores. Data moves between devices by JAX's collectives and lax.ppermute only.
A program may use at most 128 MiB of HBM per device.

v0:
```python
import jax
import jax.numpy as jnp
from jax import lax
from jax.sharding import PartitionSpec as P


def per_device(loadings, scales, cov):
    n_loads, width = loadings.shape
    groups = scales.shape[1]
    team_size = lax.axis_size("team")
    blk_size = lax.axis_size("blk")
    scaled = (
        (
            loadings.astype(jnp.float32).reshape(n_loads, groups, width // groups)
            * scales.astype(jnp.float32)[:, :, None]
        )
        .reshape(n_loads, width)
        .astype(jnp.bfloat16)
    )
    pairs = []
    for b in range(blk_size):
        c, d = divmod(b, team_size)
        for p in range(team_size):
            pairs.append((b * team_size + p, (c * team_size + p) * team_size + d))
    moved = lax.ppermute(scaled, ("blk", "team"), pairs)
    gathered = lax.all_gather(moved, "blk", axis=1, tiled=True)
    stops = cov.shape[1]
    gathered = gathered.reshape(n_loads, stops, cov.shape[3])
    cov_local = cov[:, :, 0, :]
    part = lax.dot_general(
        gathered, cov_local, (((1, 2), (1, 2)), ((), ())), preferred_element_type=jnp.float32
    )
    return lax.psum(part, "team")


def solution(mesh):
    placed = (P(None, ("blk", "team")), P(None, ("blk", "team")), P("blk", None, "team", None))
    return jax.shard_map(
        per_device, mesh=mesh, in_specs=placed, out_specs=P(None, "blk"), check_vma=False
    )
```

profile of v0, /device:TPU:1, one launch (start us, length us, event | category | flops | bytes accessed | tf_op | source)
XLA Modules:
  0.0 395.1 jit_solution(3153705874606790821)
XLA Ops:
  6.5 0.0 all-gather.2.cloned.1.call-start
  6.5 0.8 copy.6
  7.3 0.1 mul.11
  7.4 0.8 fusion.9
  8.3 4.9 %collective-permute-start = (bf16[64,384]{1,0:T(8,128)(2,1)S(1)}, bf16[64,384]{1,0:T(8,128)(2,1)S(1)}, u32[]{:S(2)}, u32[]{:S(2)}) collective-permute-start(bf16[64,384]{1,0:T(8,128)(2,1)S(1)} %fusion.9), channel_id=1, source_target_pairs={{0,0},{1,4},{2,8},{3,12},{4,1},{5,5},{6,9},{7,13},{8,2},{9,6},{10,... | collective-permute-start | bytes 147464 | tf_op jit(solution)/shard_map/ppermute | solution.py:25
  13.2 1.8 collective-permute-done
  15.0 0.0 copy-start
  15.0 0.6 copy-done
  15.6 0.0 all-gather.2.cloned.1.call-update
  15.6 0.0 all-reduce.2.cloned.1.call-start
  15.7 265.7 %all-gather.2.cloned.1.call-done = bf16[64,24576]{1,0:T(8,128)(2,1)} async-done(((bf16[64,384]{1,0:T(8,128)(2,1)}), bf16[64,24576]{1,0:T(8,128)(2,1)}) %all-gather.2.cloned.1.call-update) | async-done | bytes 3145744 | tf_op jit(solution)/shard_map/all_gather | solution.py:26
  281.4 19.6 %fusion.4 = f32[64,256]{1,0:T(8,128)} fusion(bf16[256,16,1536]{2,1,0:T(8,128)(2,1)} %bitcast.15, bf16[8,16,8,1536]{3,2,1,0:T(8,128)(2,1)} %bitcast.16), kind=kOutput, calls=%fused_computation.4 | convolution fusion | flops 805306368 | bytes 15794176 | tf_op jit(solution)/shard_map/dot_general | solution.py:30
  301.0 0.0 all-reduce.2.cloned.1.call-update
  301.1 85.7 %all-reduce.2.cloned.1.call-done = f32[64,256]{1,0:T(8,128)} async-done(((f32[64,256]{1,0:T(8,128)}), f32[64,256]{1,0:T(8,128)}) %all-reduce.2.cloned.1.call-update) | async-done | bytes 65552 | tf_op jit(solution)/shard_map/psum | solution.py:33
  386.7 1.5 copy.23
Async XLA Ops:
  6.5 274.9 %all-gather.2.cloned.1.call-start = ((), (), s32[]{:S(2)}) async-start(), calls=%async_computation | async-start | bytes 3194880 | tf_op jit(solution)/shard_map/all_gather | solution.py:26
  8.3 6.7 %collective-permute-start = (bf16[64,384]{1,0:T(8,128)(2,1)S(1)}, bf16[64,384]{1,0:T(8,128)(2,1)S(1)}, u32[]{:S(2)}, u32[]{:S(2)}) collective-permute-start(bf16[64,384]{1,0:T(8,128)(2,1)S(1)} %fusion.9), channel_id=1, source_target_pairs={{0,0},{1,4},{2,8},{3,12},{4,1},{5,5},{6,9},{7,13},{8,2},{9,6},{10,... | collective-permute-start | bytes 147464 | tf_op jit(solution)/shard_map/ppermute | solution.py:25
  15.0 0.6 copy-start
  15.6 371.1 %all-reduce.2.cloned.1.call-start = ((), (), s32[]{:S(2)}) async-start(), calls=%async_computation.1 | async-start | bytes 131072 | tf_op jit(solution)/shard_map/psum | solution.py:33
Sparse Core Ops, SparseCore 0:
  15.7 265.6 all-gather.1
  301.2 85.5 all-reduce.1
where the time goes:
time: 395 us
  waiting for transfers between devices  353 us (89%)
  matrix products  19.6 us (5%)
  between operations  13.4 us (3%)
  starting transfers between devices  4.98 us (1%)
    all_gather x1, waiting for transfers between devices, per_device(): gathered = lax.all_gather(moved, 'blk', axis=1, tiled=True)  266 us
    psum x1, waiting for transfers between devices, per_device(): return lax.psum(part, 'team')  85.7 us
    dot_general x1, matrix products, per_device(): lax.dot_general(gathered, cov_local, (((1, 2), (1, 2)), ((), ())), prefer...  19.6 us
  transfers between devices with their start and end apart: 3, of which 3 were waited for; matrix products, arithmetic and copies ran while one was open for 0% of the time, Pallas kernels for 0%

commit v1 on v0

--- a/solution.py
+++ b/solution.py
@@ -23,7 +23,10 @@
         for p in range(team_size):
             pairs.append((b * team_size + p, (c * team_size + p) * team_size + d))
     moved = lax.ppermute(scaled, ("blk", "team"), pairs)
-    gathered = lax.all_gather(moved, "blk", axis=1, tiled=True)
+    peers = lax.axis_size("blk")
+    blocks = jnp.stack([moved for _ in range(peers)])
+    blocks = lax.all_to_all(blocks, "blk", split_axis=0, concat_axis=0)
+    gathered = jnp.concatenate(blocks, axis=1)
     stops = cov.shape[1]
     gathered = gathered.reshape(n_loads, stops, cov.shape[3])
     cov_local = cov[:, :, 0, :]

time: 395 us -> 184 us (0.47)
  waiting for transfers between devices: 353 us -> 51.2 us
  blocking collectives: 0 us -> 83.2 us
  local copies, waits for them, and re-layouts: 2.99 us -> 7.92 us
    all_gather x1 -> x0, waiting for transfers between devices: 266 us -> none  [per_device(): gathered = lax.all_gather(moved, 'blk', axis=1, tiled=True)]
    all_to_all x0 -> x1, blocking collectives: none -> 83.2 us  [per_device(): blocks = lax.all_to_all(blocks, 'blk', split_axis=0, concat_axis=0)]
    psum x1, waiting for transfers between devices: 85.7 us -> 49.4 us  [per_device(): return lax.psum(part, 'team')]
  transfers between devices with their start and end apart: 3 -> 2, of which waited for: 3 -> 2; matrix products, arithmetic and copies ran while one was open for 0% -> 0% of each run, Pallas kernels for 0% -> 0%
where the time goes in v1:
time: 184 us
  blocking collectives  83.2 us (45%)
  waiting for transfers between devices  51.2 us (28%)
  matrix products  22.7 us (12%)
  between operations  13.4 us (7%)
  local copies, waits for them, and re-layouts  7.92 us (4%)
  starting transfers between devices  4.94 us (3%)
    all_to_all x1, blocking collectives, per_device(): blocks = lax.all_to_all(blocks, 'blk', split_axis=0, concat_axis=0)  83.2 us
    psum x1, waiting for transfers between devices, per_device(): return lax.psum(part, 'team')  49.4 us
    dot_general x1, matrix products, per_device(): lax.dot_general(gathered, cov_local, (((1, 2), (1, 2)), ((), ())), prefer...  22.7 us
    ppermute x1, starting transfers between devices, per_device(): moved = lax.ppermute(scaled, ('blk', 'team'), pairs)  4.94 us
  transfers between devices with their start and end apart: 2, of which 2 were waited for; matrix products, arithmetic and copies ran while one was open for 0% of the time, Pallas kernels for 0%

profile of v1, /device:TPU:1, one launch (start us, length us, event | category | flops | bytes accessed | tf_op | source)
XLA Modules:
  0.0 184.1 jit_solution(7296556760959173800)
XLA Ops:
  6.5 0.0 all-reduce.2.cloned.1.call-start
  6.5 0.8 copy.9
  7.3 0.1 mul.11
  7.4 0.8 fusion.8
  8.3 4.9 %collective-permute-start = (bf16[64,384]{1,0:T(8,128)(2,1)S(1)}, bf16[64,384]{1,0:T(8,128)(2,1)S(1)}, u32[]{:S(2)}, u32[]{:S(2)}) collective-permute-start(bf16[64,384]{1,0:T(8,128)(2,1)S(1)} %fusion.8), channel_id=1, source_target_pairs={{0,0},{1,4},{2,8},{3,12},{4,1},{5,5},{6,9},{7,13},{8,2},{9,6},{10,... | collective-permute-start | bytes 147464 | tf_op jit(solution)/shard_map/ppermute | solution.py:25
  13.2 1.8 collective-permute-done
  15.0 0.5 stack.2
  15.5 83.2 %all_to_all.5 = bf16[64,64,384]{2,1,0:T(8,128)(2,1)S(1)} all-to-all(bf16[64,64,384]{2,1,0:T(8,128)(2,1)S(1)} %stack.2), channel_id=1, replica_groups=mesh['blk'=64,'team'=4] {'blk'}, dimensions={0} | all-to-all | bytes 6291456 | tf_op jit(solution)/shard_map/all_to_all | solution.py:28
  98.7 1.9 %copy.10 = bf16[64,64,384]{2,1,0:T(8,128)(2,1)S(1)} copy(bf16[64,64,384]{2,0,1:T(8,128)(2,1)S(1)} %bitcast.9) | data formatting | bytes 6291456 | tf_op jit(solution)/shard_map/reshape | solution.py:29
  100.5 3.2 %reshape_reshape.3 = bf16[64,16,1536]{2,1,0:T(8,128)(2,1)} reshape(bf16[64,64,384]{2,1,0:T(8,128)(2,1)S(1)} %copy.10) | data formatting | bytes 6291456 | tf_op jit(solution)/shard_map/reshape;reshape | solution.py:31
  103.7 22.7 %fusion.3 = f32[64,256]{1,0:T(8,128)} fusion(bf16[256,16,1536]{2,1,0:T(8,128)(2,1)} %bitcast.11, bf16[64,16,1536]{2,1,0:T(8,128)(2,1)} %reshape_reshape.3), kind=kOutput, calls=%fused_computation.3 | convolution fusion | flops 805306368 | bytes 15794176 | tf_op jit(solution)/shard_map/dot_general | solution.py:33
  126.4 0.0 all-reduce.2.cloned.1.call-update
  126.4 49.4 %all-reduce.2.cloned.1.call-done = f32[64,256]{1,0:T(8,128)} async-done(((f32[64,256]{1,0:T(8,128)}), f32[64,256]{1,0:T(8,128)}) %all-reduce.2.cloned.1.call-update) | async-done | bytes 65552 | tf_op jit(solution)/shard_map/psum | solution.py:36
  175.8 1.5 copy.24
Async XLA Ops:
  6.5 169.3 %all-reduce.2.cloned.1.call-start = ((), (), s32[]{:S(2)}) async-start(), calls=%async_computation.1 | async-start | bytes 131072 | tf_op jit(solution)/shard_map/psum | solution.py:36
  8.3 6.7 %collective-permute-start = (bf16[64,384]{1,0:T(8,128)(2,1)S(1)}, bf16[64,384]{1,0:T(8,128)(2,1)S(1)}, u32[]{:S(2)}, u32[]{:S(2)}) collective-permute-start(bf16[64,384]{1,0:T(8,128)(2,1)S(1)} %fusion.8), channel_id=1, source_target_pairs={{0,0},{1,4},{2,8},{3,12},{4,1},{5,5},{6,9},{7,13},{8,2},{9,6},{10,... | collective-permute-start | bytes 147464 | tf_op jit(solution)/shard_map/ppermute | solution.py:25
Sparse Core Ops, SparseCore 0:
  126.5 49.2 all-reduce.1
